TPU v7x, 512 devices: a whole 4x4x16 slice. The times are simulated.
512 devices in a mesh: mx: 32 (over z, core), my: 4 (over y), layer: 4 (over x).
Axes of the slice: x: 4, y: 4, z: 16, core: 2. Of those that a mesh axis runs over, the one named last changes fastest.
Arguments:
- ssa_velocity: float32 [2, 2048, 1024], P(None, 'mx', 'my'), may hold values from -6 to 6
- shelf_viscosity: float32 [2048, 1024], P('mx', 'my'), may hold values from 0.3 to 3
- basal_friction: float32 [2048, 1024], P('mx', 'my'), may hold values from 0.1 to 3
- driving_stress: float32 [2, 2048, 1024], P(None, 'mx', 'my'), may hold values from -6 to 6
- stokes_velocity: float32 [3, 12, 512, 1024], P(None, 'layer', 'mx', 'my'), may hold values from -6 to 6
- ice_viscosity: float32 [12, 512, 1024], P('layer', 'mx', 'my'), may hold values from 0.3 to 3
- body_force: float32 [3, 12, 512, 1024], P(None, 'layer', 'mx', 'my'), may hold values from -6 to 6
- diagonals: int32 [512, 1024], P('mx', 'my'), may hold values 0 or 1
- element_matrix: float32 [18, 18], replicated, may hold values from -0.1 to 1.5, as said below
- iface_columns: int32 [128, 9, 128], P(('mx', 'my')), may hold values from -1 to 4095, as said below
- iface_nodes: int32 [128, 9, 128], P(('mx', 'my')), may hold values from -1 to 16383, as said below
Outputs:
- coupled_residual: float32 [2, 2048, 1024], P(None, 'mx', 'my')
- stokes_residual: float32 [3, 12, 512, 1024], P(None, 'layer', 'mx', 'my')
Inputs may be any that keep to these rules, and one draw needn't show every extreme that they name: `iface_columns`: slots toward blocks outside the map are empty; in each block and direction the live slots come first; all 128 slots toward a block's own direction (d = 4) are live; the live columns of one block are distinct. `iface_nodes`: slot (o, d, k) is live exactly where its partner slot (s, 8 - d, k) of iface_columns is live, s the block at offset d from o, and then names a node of o's 64 x 256 block (row-major). `element_matrix`: the diagonal dominates each row.
All inputs are finite; a program needn't handle non-finite values. No bound on the sum of `diagonals` on one device may be relied on, other than what follows from the above.
Results may differ from a plain program's by a relative error of at most 0.0001.
Values sent between devices are 32-bit elements; how exact they have to be, the bound alone decides.
No kernel may reach another device: no remote copies, remote signals or barrier semaphores. Data moves between devices by JAX's collectives and lax.ppermute only.
A program may use at most 64 MiB of HBM per device.

v0:
```python
import jax
import jax.numpy as jnp
from jax import lax
from jax.sharding import PartitionSpec as P


def with_halo(array, sides, width):
    for axis, dim in sides:
        devices, length = (lax.axis_size(axis), array.shape[dim])
        up = [(i, (i + 1) % devices) for i in range(devices - 1)]
        down = [(j, i) for i, j in up]
        last = lax.slice_in_dim(array, length - width, length, axis=dim)
        initial = lax.slice_in_dim(array, 0, width, axis=dim)
        before = lax.ppermute(last, axis, up)
        after = lax.ppermute(initial, axis, down)
        array = jnp.concatenate([before, array, after], axis=dim)
    return array


def cell_dx(plane):
    return 0.5 * (plane[1:, :-1] + plane[1:, 1:] - (plane[:-1, :-1] + plane[:-1, 1:]))


def cell_dy(plane):
    return 0.5 * (plane[:-1, 1:] + plane[1:, 1:] - (plane[:-1, :-1] + plane[1:, :-1]))


def shelf_residual(padded, friction, driving):
    u_field = padded[0]
    v_field = padded[1]
    h_field = padded[2]
    du_dx = cell_dx(u_field)
    du_dy = cell_dy(u_field)
    dv_dx = cell_dx(v_field)
    dv_dy = cell_dy(v_field)
    h_cell = 0.25 * (h_field[1:, :-1] + h_field[1:, 1:] + h_field[:-1, :-1] + h_field[:-1, 1:])
    tau_xx = h_cell * (4.0 * du_dx + 2.0 * dv_dy)
    tau_yy = h_cell * (4.0 * dv_dy + 2.0 * du_dx)
    tau_xy = h_cell * (du_dy + dv_dx)
    res_x = cell_dx(tau_xx) + cell_dy(tau_xy) - friction * u_field[1:-1, 1:-1] - driving[0]
    res_y = cell_dy(tau_yy) + cell_dx(tau_xy) - friction * v_field[1:-1, 1:-1] - driving[1]
    return jnp.stack([res_x, res_y])


def triangle(stiffness, lows, ups, weight):
    values = jnp.stack(
        [plane[comp] for group in (lows, ups) for comp in range(3) for plane in group]
    )
    viscous = (
        (lows[0][3] + lows[1][3] + lows[2][3] + ups[0][3] + ups[1][3] + ups[2][3]) / 6.0 * weight
    )
    response = (
        jnp.einsum("ab,bxy->axy", stiffness, values, precision=lax.Precision.HIGHEST) * viscous
    )
    return response.reshape((2, 3, 3) + response.shape[1:])


def cell_terms(lower, upper, flag_cells, stiffness, weight):
    low_a, low_b, low_c, low_d = (
        lower[:, :-1, :-1],
        lower[:, 1:, :-1],
        lower[:, :-1, 1:],
        lower[:, 1:, 1:],
    )
    up_a, up_b, up_c, up_d = (
        upper[:, :-1, :-1],
        upper[:, 1:, :-1],
        upper[:, :-1, 1:],
        upper[:, 1:, 1:],
    )
    main_diag = (flag_cells == 0)[None]
    low_far = jnp.where(main_diag, low_d, low_c)
    up_far = jnp.where(main_diag, up_d, up_c)
    low_near = jnp.where(main_diag, low_a, low_b)
    up_near = jnp.where(main_diag, up_a, up_b)
    tri_one = triangle(stiffness, (low_a, low_b, low_far), (up_a, up_b, up_far), weight)
    tri_two = triangle(stiffness, (low_near, low_d, low_c), (up_near, up_d, up_c), weight)
    result = []
    for height in range(2):
        resp_one = tri_one[height]
        resp_two = tri_two[height]
        corner_a = resp_one[:, 0] + jnp.where(main_diag, resp_two[:, 0], 0.0)
        corner_b = resp_one[:, 1] + jnp.where(main_diag, 0.0, resp_two[:, 0])
        corner_c = resp_two[:, 2] + jnp.where(main_diag, 0.0, resp_one[:, 2])
        corner_d = resp_two[:, 1] + jnp.where(main_diag, resp_one[:, 2], 0.0)
        result.append((corner_a, corner_b, corner_c, corner_d))
    return (result[0], result[1])


def add_corners(total, extra):
    if total is None:
        return extra
    return tuple((first_term + other_term for first_term, other_term in zip(total, extra)))


def scaled_by(corners, factor):
    return tuple((member * factor for member in corners))


def own_nodes(corners):
    corner_a, corner_b, corner_c, corner_d = corners
    return corner_a[:, 1:, 1:] + corner_b[:, :-1, 1:] + corner_c[:, 1:, :-1] + corner_d[:, :-1, :-1]


def per_device(
    ssa_velocity,
    shelf_viscosity,
    basal_friction,
    driving_stress,
    stokes_velocity,
    ice_viscosity,
    body_force,
    diagonals,
    element_matrix,
    iface_columns,
    iface_nodes,
):
    row_count = ssa_velocity.shape[1]
    col_count = ssa_velocity.shape[2]
    stacked = jnp.concatenate([ssa_velocity, shelf_viscosity[None]], 0)
    padded = with_halo(stacked, (("mx", 1), ("my", 2)), 1)
    shelf_res = shelf_residual(padded, basal_friction, driving_stress)
    owner_nodes = iface_nodes[0]
    node_live = owner_nodes >= 0
    flat_vel = ssa_velocity.reshape(2, row_count * col_count)
    outgoing = jnp.where(node_live[None], flat_vel[:, jnp.maximum(owner_nodes, 0)], 0.0)
    slot_count = outgoing.shape[2]
    grid_out = outgoing.reshape(2, 3, 3, slot_count)
    extended = with_halo(grid_out, (("mx", 1), ("my", 2)), 1)
    returned = extended[:, 0::2, 0::2].reshape(2, 9, slot_count)
    depth_count = stokes_velocity.shape[1]
    block_x = stokes_velocity.shape[2]
    block_y = stokes_velocity.shape[3]
    column_count = block_x * block_y
    columns = iface_columns[0]
    col_live = columns >= 0
    target = jnp.where(col_live, columns, column_count).reshape(-1)
    placed = (
        jnp.zeros((2, column_count + 1), jnp.float32)
        .at[:, target]
        .add(returned.reshape(2, -1))[:, :column_count]
    )
    marked = jnp.zeros((column_count + 1,), jnp.float32).at[target].add(1.0)[:column_count] > 0.0
    uv_part = jnp.where(
        marked.reshape(1, 1, block_x, block_y),
        placed.reshape(2, 1, block_x, block_y),
        stokes_velocity[:2],
    )
    stokes_field = jnp.concatenate([uv_part, stokes_velocity[2:3], ice_viscosity[None]], 0)
    planes = jnp.concatenate(
        [
            stokes_field.reshape(4 * depth_count, block_x, block_y),
            diagonals.astype(jnp.float32)[None],
        ],
        0,
    )
    widened = with_halo(planes, (("mx", 1), ("my", 2)), 1)
    flag_cells = widened[-1, :-1, :-1]
    field_ext = widened[:-1].reshape(4, depth_count, block_x + 2, block_y + 2)
    count_x = lax.axis_size("mx")
    count_y = lax.axis_size("my")
    place_x = lax.axis_index("mx")
    place_y = lax.axis_index("my")
    global_x = place_x * block_x + jnp.arange(block_x + 1, dtype=jnp.int32) - 1
    global_y = place_y * block_y + jnp.arange(block_y + 1, dtype=jnp.int32) - 1
    valid_x = (global_x >= 0) & (global_x <= count_x * block_x - 2)
    valid_y = (global_y >= 0) & (global_y <= count_y * block_y - 2)
    weight = (valid_x[:, None] & valid_y[None, :]).astype(jnp.float32)
    layer_index = lax.axis_index("layer")
    layer_count = lax.axis_size("layer")
    below_live = (layer_index > 0).astype(jnp.float32)
    above_live = (layer_index < layer_count - 1).astype(jnp.float32)
    extended_layers = with_halo(field_ext, (("layer", 1),), 1)
    collected = [None for height in range(depth_count)]
    for height in range(depth_count + 1):
        lower_part, upper_part = cell_terms(
            extended_layers[:, height],
            extended_layers[:, height + 1],
            flag_cells,
            element_matrix,
            weight,
        )
        if height > 0:
            if height == depth_count:
                lower_part = scaled_by(lower_part, above_live)
            collected[height - 1] = add_corners(collected[height - 1], lower_part)
        if height < depth_count:
            if height == 0:
                upper_part = scaled_by(upper_part, below_live)
            collected[height] = add_corners(collected[height], upper_part)
    owned = [own_nodes(corners) for corners in collected]
    stokes_residual = jnp.stack(owned, axis=1) - body_force
    depth_sum = jnp.sum(stokes_residual[:2], axis=1).reshape(2, column_count)
    bucket = jnp.where(col_live[None], depth_sum[:, jnp.maximum(columns, 0)], 0.0)
    depth_total = lax.psum(bucket, "layer")
    grid_back = depth_total.reshape(2, 3, 3, slot_count)
    extended_back = with_halo(grid_back, (("mx", 1), ("my", 2)), 1)
    at_owner = extended_back[:, 0::2, 0::2].reshape(2, 9, slot_count)
    node_index = jnp.where(node_live, owner_nodes, row_count * col_count).reshape(-1)
    node_force = (
        jnp.zeros((2, row_count * col_count + 1), jnp.float32)
        .at[:, node_index]
        .add(at_owner.reshape(2, -1))
    )
    node_force = node_force[:, : row_count * col_count].reshape(2, row_count, col_count)
    coupled_residual = shelf_res - node_force
    return (coupled_residual, stokes_residual)


def solution(mesh):
    return jax.shard_map(
        per_device,
        mesh=mesh,
        in_specs=(
            P(None, "mx", "my"),
            P("mx", "my"),
            P("mx", "my"),
            P(None, "mx", "my"),
            P(None, "layer", "mx", "my"),
            P("layer", "mx", "my"),
            P(None, "layer", "mx", "my"),
            P("mx", "my"),
            P(),
            P(("mx", "my"), None, None),
            P(("mx", "my"), None, None),
        ),
        out_specs=(P(None, "mx", "my"), P(None, "layer", "mx", "my")),
        check_vma=False,
    )
```

profile of v0, /device:TPU:97, one launch (start us, length us, event | category | flops | bytes accessed | tf_op | source)
XLA Modules:
  0.0 201.1 jit_solution(2747815549716672843)
XLA Ops:
  0.7 0.8 maximum_reduce_fusion.1
  1.5 0.7 compare_reduce_fusion
  2.9 5.5 %copy.172 = f32[2,64,256]{0,2,1:T(8,128)} copy(f32[2,64,256]{2,1,0:T(8,128)} %param.11) | data formatting | bytes 262144 | tf_op args[0]
  9.0 5.8 %gather_fusion = f32[1152,2]{1,0:T(8,128)S(1)} fusion(f32[2,16384]{0,1:T(8,128)} %bitcast.297, s32[2048]{0:T(1024)S(1)} %get-tuple-element.199), kind=kCustom, calls=%fused_computation | custom fusion | bytes 23040 | tf_op jit(solution)/shard_map/gather | solution.py:126
  15.1 5.3 %collective-permute-start.4 = (f32[2,1,3,128]{3,0,2,1:T(2,128)S(1)}, f32[2,1,3,128]{3,0,2,1:T(2,128)S(1)}, u32[]{:S(2)}, u32[]{:S(2)}) collective-permute-start(f32[2,1,3,128]{3,0,2,1:T(2,128)S(1)} %get-tuple-element.196), channel_id=1, source_target_pairs={{0,16},{16,32},{32,48},{48,64},{64,80},{80,96},{96,112},{112,128},... | collective-permute-start | bytes 9224 | tf_op jit(solution)/shard_map/ppermute | solution.py:14
  20.5 1.9 collective-permute-start.5
  22.4 4.9 %collective-permute-start = (f32[3,1,256]{2,1,0:T(1,128)S(1)}, f32[3,1,256]{2,1,0:T(1,128)S(1)}, u32[]{:S(2)}, u32[]{:S(2)}) collective-permute-start(f32[3,1,256]{2,1,0:T(1,128)S(1)} %get-tuple-element.76), channel_id=1, source_target_pairs={{0,16},{16,32},{32,48},{48,64},{64,80},{80,96},{96,112},{112,128},... | collective-permute-start | bytes 9224 | tf_op jit(solution)/shard_map/ppermute | solution.py:14
  27.3 1.9 collective-permute-start.1
  29.9 8.7 %scatter_custom_fusion = f32[4097]{0:T(1024)S(1)} fusion(s32[1152]{0:T(1024)S(1)} %fusion.75, f32[1152]{0:T(1024)S(1)} %broadcast.299, f32[]{:T(128)} %constant.32.clone.1), kind=kCustom, calls=%fused_computation.252 | custom fusion | flops 1152 | bytes 16392 | tf_op jit(solution)/shard_map/scatter-add | solution.py:143
  39.4 2.8 %collective-permute-start.2 = (f32[3,66,1]{2,1,0:T(8,128)S(1)}, f32[3,66,1]{2,1,0:T(8,128)S(1)}, u32[]{:S(2)}, u32[]{:S(2)}) collective-permute-start(f32[3,66,1]{2,1,0:T(8,128)S(1)} %get-tuple-element.74), channel_id=1, source_target_pairs={{0,4},{4,8},{8,12},{1,5},{5,9},{9,13},{2,6},{6,10},{10,14},{3,7},{... | collective-permute-start | bytes 2384 | tf_op jit(solution)/shard_map/ppermute | solution.py:14
  42.2 1.3 collective-permute-start.3
  43.5 4.0 %collective-permute-start.6 = (f32[2,5,1,128]{3,0,2,1:T(2,128)S(1)}, f32[2,5,1,128]{3,0,2,1:T(2,128)S(1)}, u32[]{:S(2)}, u32[]{:S(2)}) collective-permute-start(f32[2,5,1,128]{3,0,2,1:T(2,128)S(1)} %get-tuple-element.182), channel_id=1, source_target_pairs={{0,4},{4,8},{8,12},{1,5},{5,9},{9,13},{2,6},{6,10},{10,14},{3,7},{... | collective-permute-start | bytes 15368 | tf_op jit(solution)/shard_map/ppermute | solution.py:14
  47.5 1.3 collective-permute-start.7
  49.1 2.8 %collective-permute-done.7 = f32[2,5,1,128]{3,0,2,1:T(2,128)S(1)} collective-permute-done((f32[2,5,1,128]{3,0,2,1:T(2,128)S(1)}, f32[2,5,1,128]{3,0,2,1:T(2,128)S(1)}, u32[]{:S(2)}, u32[]{:S(2)}) %collective-permute-start.7) | collective-permute-done | bytes 5152 | tf_op jit(solution)/shard_map/ppermute | solution.py:15
  52.2 10.6 %scatter_custom_fusion.1 = f32[2,4097]{0,1:T(8,128)S(1)} fusion(s32[1152]{0:T(1024)S(1)} %fusion.75, f32[1152,2]{1,0:T(8,128)S(1)} %copy.174, f32[]{:T(128)} %constant.32.clone.1), kind=kCustom, calls=%fused_computation.23 | custom fusion | flops 2304 | bytes 32780 | tf_op jit(solution)/shard_map/scatter-add | solution.py:141
  62.8 1.5 slice.1284
  64.3 2.2 %copy.175 = f32[2,16,256]{2,1,0:T(8,128)S(1)} copy(f32[2,16,256]{0,2,1:T(8,128)} %bitcast.298) | data formatting | bytes 65536 | tf_op jit(solution)/shard_map/jit(_where)/broadcast_in_dim | solution.py:144
  66.7 7.0 %collective-permute-start.8 = (f32[13,1,256]{2,0,1:T(8,128)S(1)}, f32[13,1,256]{2,0,1:T(8,128)S(1)}, u32[]{:S(2)}, u32[]{:S(2)}) collective-permute-start(f32[13,1,256]{2,0,1:T(8,128)S(1)} %get-tuple-element.64), channel_id=1, source_target_pairs={{0,16},{16,32},{32,48},{48,64},{64,80},{80,96},{96,112},{112,128},... | collective-permute-start | bytes 39944 | tf_op jit(solution)/shard_map/ppermute | solution.py:14
  73.6 1.9 collective-permute-start.9
  75.8 4.1 %collective-permute-done.9 = f32[13,1,256]{2,0,1:T(8,128)S(1)} collective-permute-done((f32[13,1,256]{2,0,1:T(8,128)S(1)}, f32[13,1,256]{2,0,1:T(8,128)S(1)}, u32[]{:S(2)}, u32[]{:S(2)}) %collective-permute-start.9) | collective-permute-done | bytes 13344 | tf_op jit(solution)/shard_map/ppermute | solution.py:15
  80.1 2.7 %collective-permute-start.10 = (f32[13,18,1]{2,0,1:T(8,128)S(1)}, f32[13,18,1]{2,0,1:T(8,128)S(1)}, u32[]{:S(2)}, u32[]{:S(2)}) collective-permute-start(f32[13,18,1]{2,0,1:T(8,128)S(1)} %get-tuple-element.62), channel_id=1, source_target_pairs={{0,4},{4,8},{8,12},{1,5},{5,9},{9,13},{2,6},{6,10},{10,14},{3,7},{... | collective-permute-start | bytes 2816 | tf_op jit(solution)/shard_map/ppermute | solution.py:14
  82.8 1.3 collective-permute-start.11
  84.9 3.8 %collective-permute-done.11 = f32[13,18,1]{2,0,1:T(8,128)S(1)} collective-permute-done((f32[13,18,1]{2,0,1:T(8,128)S(1)}, f32[13,18,1]{2,0,1:T(8,128)S(1)}, u32[]{:S(2)}, u32[]{:S(2)}) %collective-permute-start.11) | collective-permute-done | bytes 968 | tf_op jit(solution)/shard_map/ppermute | solution.py:15
  89.2 3.1 %collective-permute-start.12 = (f32[4,1,18,258]{3,0,2,1:T(4,128)S(1)}, f32[4,1,18,258]{3,0,2,1:T(4,128)S(1)}, u32[]{:S(2)}, u32[]{:S(2)}) collective-permute-start(f32[4,1,18,258]{3,0,2,1:T(4,128)S(1)} %copy.245), channel_id=1, source_target_pairs={{0,1},{1,2},{2,3},{4,5},{5,6},{6,7},{8,9},{9,10},{10,11},{12,13},{... | collective-permute-start | bytes 222920 | tf_op jit(solution)/shard_map/ppermute | solution.py:14
  93.6 1.5 collective-permute-start.13
  95.6 1.1 fusion.87
  98.9 1.0 and_select_fusion.5
  100.1 1.2 and_select_fusion.3
  101.6 1.1 fusion.89
  103.4 1.8 and_select_fusion.1
  105.9 2.2 %stack.48 = f32[18,17,257]{2,0,1:T(8,128)S(1)} concatenate(f32[1,17,257]{2,0,1:T(1,128)} %get-tuple-element.106, f32[1,17,257]{2,0,1:T(1,128)} %get-tuple-element.105, f32[1,17,257]{2,0,1:T(1,128)} %get-tuple-element.152, f32[1,17,257]{2,0,1:T(1,128)} %get-tuple-element.103, f32[1,17,257]{2,0,1:T(1,128)S(1)} %get-tuple-element.102, f32[1,17,257]{2,0,1:T(1,128)} %get-tuple-element.151, ...), dimensions={0} | concatenate | bytes 629136 | tf_op jit(solution)/shard_map/stack | solution.py:46
  108.9 0.7 slice_bitcast_fusion.35
  109.7 0.8 stack.49
  112.0 0.8 stack.50
  113.6 0.7 slice_bitcast_fusion.33
  114.3 0.7 copy.302
  115.1 0.8 stack.51
  118.3 0.7 slice_bitcast_fusion.22
  119.0 0.7 copy.301
  119.8 1.0 stack.53
  122.3 0.7 copy.300
  123.0 1.5 stack.54
  126.1 0.7 copy.299
  126.8 2.3 %stack.56 = f32[18,17,257]{2,0,1:T(8,128)S(1)} concatenate(f32[1,17,257]{2,0,1:T(1,128)S(1)} %get-tuple-element.142, f32[1,17,257]{2,0,1:T(1,128)S(1)} %get-tuple-element.141, f32[1,17,257]{2,0,1:T(1,128)S(1)} %copy-done.5, f32[1,17,257]{2,0,1:T(1,128)S(1)} %get-tuple-element.140, f32[1,17,257]{2,0,1:T(1,128)S(1)} %get-tuple-element.139, f32[1,17,257]{2,0,1:T(1,128)S(1)} %get-tuple-element.166, ...), dimensions={0} | concatenate | bytes 629136 | tf_op jit(solution)/shard_map/stack | solution.py:46
  131.4 0.7 copy.298
  132.1 2.3 %stack.57 = f32[18,17,257]{2,0,1:T(8,128)S(1)} concatenate(f32[1,17,257]{2,0,1:T(1,128)S(1)} %get-tuple-element.176, f32[1,17,257]{2,0,1:T(1,128)S(1)} %get-tuple-element.137, f32[1,17,257]{2,0,1:T(1,128)S(1)} %get-tuple-element.118, f32[1,17,257]{2,0,1:T(1,128)S(1)} %get-tuple-element.175, f32[1,17,257]{2,0,1:T(1,128)S(1)} %get-tuple-element.117, ...), dimensions={0} | concatenate | bytes 629136 | tf_op jit(solution)/shard_map/stack | solution.py:46
  135.4 1.3 fusion.39
  136.8 1.3 fusion.47
  138.1 1.1 fusion.27
  139.3 0.9 maximum_subtract_fusion
  140.8 2.9 %gather_fusion.1 = f32[1152,2]{1,0:T(8,128)S(1)} fusion(f32[2,4096]{0,1:T(8,128)S(1)} %bitcast.305, s32[2048]{0:T(1024)} %get-tuple-element.198), kind=kCustom, calls=%fused_computation.1 | custom fusion | bytes 23040 | tf_op jit(solution)/shard_map/gather | solution.py:194
  143.7 0.9 select_bitcast_fusion
  144.8 9.6 %psum.7 = f32[2,3,3,128]{3,0,2,1:T(2,128)S(1)} all-reduce(f32[2,3,3,128]{3,0,2,1:T(2,128)S(1)} %bitcast.339), channel_id=1, replica_groups=mesh['mx'=32,'my'=4,'layer'=4] {'layer'}, use_global_device_ids=true, to_apply=%region_3.4 | all-reduce | flops 2304 | bytes 18432 | tf_op jit(solution)/shard_map/psum | solution.py:195
  154.4 5.9 %collective-permute-start.14 = (f32[2,1,3,128]{3,0,2,1:T(2,128)S(1)}, f32[2,1,3,128]{3,0,2,1:T(2,128)S(1)}, u32[]{:S(2)}, u32[]{:S(2)}) collective-permute-start(f32[2,1,3,128]{3,0,2,1:T(2,128)S(1)} %get-tuple-element.185), channel_id=1, source_target_pairs={{0,16},{16,32},{32,48},{48,64},{64,80},{80,96},{96,112},{112,128},... | collective-permute-start | bytes 9224 | tf_op jit(solution)/shard_map/ppermute | solution.py:14
  160.4 1.0 fusion.15
  161.4 1.9 collective-permute-start.15
  163.3 4.2 %collective-permute-done.15 = f32[2,1,3,128]{3,0,2,1:T(2,128)S(1)} collective-permute-done((f32[2,1,3,128]{3,0,2,1:T(2,128)S(1)}, f32[2,1,3,128]{3,0,2,1:T(2,128)S(1)}, u32[]{:S(2)}, u32[]{:S(2)}) %collective-permute-start.15) | collective-permute-done | bytes 3104 | tf_op jit(solution)/shard_map/ppermute | solution.py:15
  167.5 3.3 %collective-permute-start.16 = (f32[2,5,1,128]{3,0,2,1:T(2,128)S(1)}, f32[2,5,1,128]{3,0,2,1:T(2,128)S(1)}, u32[]{:S(2)}, u32[]{:S(2)}) collective-permute-start(f32[2,5,1,128]{3,0,2,1:T(2,128)S(1)} %get-tuple-element.180), channel_id=1, source_target_pairs={{0,4},{4,8},{8,12},{1,5},{5,9},{9,13},{2,6},{6,10},{10,14},{3,7},{... | collective-permute-start | bytes 15368 | tf_op jit(solution)/shard_map/ppermute | solution.py:14
  170.8 1.3 collective-permute-start.17
  172.1 1.0 fusion.21
  173.8 1.4 collective-permute-done.17
  175.5 14.0 %scatter_custom_fusion.2 = f32[2,16385]{0,1:T(8,128)} fusion(s32[1152]{0:T(1024)} %fusion.74, f32[1152,2]{1,0:T(8,128)S(1)} %copy.231, f32[]{:T(128)} %constant.32.clone.1), kind=kCustom, calls=%fused_computation.5 | custom fusion | flops 2304 | bytes 131592 | tf_op jit(solution)/shard_map/scatter-add | solution.py:203
  189.5 5.7 %slice.1543 = f32[2,16384]{0,1:T(8,128)} slice(f32[2,16385]{0,1:T(8,128)} %scatter_custom_fusion.2), slice={[0:2], [0:16384]} | slice | bytes 262144 | tf_op jit(solution)/shard_map/slice | solution.py:205
  195.2 5.2 %copy.232 = f32[2,64,256]{2,1,0:T(8,128)S(1)} copy(f32[2,64,256]{0,2,1:T(8,128)} %bitcast.284) | data formatting | bytes 262144 | tf_op jit(solution)/shard_map/reshape | solution.py:205
  (181 shorter events, 25.0 us)
Async XLA Ops:
  0.6 107.5 %copy-start = (f32[18,18]{1,0:T(8,128)S(1)}, f32[18,18]{1,0:T(8,128)}, u32[]{:S(2)}) copy-start(f32[18,18]{1,0:T(8,128)} %param.19) | copy-start | bytes 3892
  0.6 28.6 %copy-start.23 = (s32[1,9,128]{2,0,1:T(1,128)S(1)}, s32[1,9,128]{2,0,1:T(1,128)}, u32[]{:S(2)}) copy-start(s32[1,9,128]{2,0,1:T(1,128)} %param.21) | copy-start | bytes 13828
  0.7 28.6 %copy-start.22 = (s32[1,9,128]{2,0,1:T(1,128)S(1)}, s32[1,9,128]{2,0,1:T(1,128)}, u32[]{:S(2)}) copy-start(s32[1,9,128]{2,0,1:T(1,128)} %param.20) | copy-start | bytes 13828
  0.7 21.7 %copy-start.1 = (f32[2,64,256]{2,1,0:T(8,128)S(1)}, f32[2,64,256]{2,1,0:T(8,128)}, u32[]{:S(2)}) copy-start(f32[2,64,256]{2,1,0:T(8,128)} %param.11) | copy-start | bytes 393220
  0.7 21.7 %copy-start.2 = (f32[64,256]{1,0:T(8,128)S(1)}, f32[64,256]{1,0:T(8,128)}, u32[]{:S(2)}) copy-start(f32[64,256]{1,0:T(8,128)} %param.12) | copy-start | bytes 196612
  0.7 38.0 %copy-start.24 = (s32[16,256]{1,0:T(8,128)S(1)}, s32[16,256]{1,0:T(8,128)}, u32[]{:S(2)}) copy-start(s32[16,256]{1,0:T(8,128)} %param.18) | copy-start | bytes 49156
  8.4 58.0 %copy-start.10 = (f32[3,3,16,256]{3,2,1,0:T(8,128)S(1)}, f32[3,3,16,256]{3,2,1,0:T(8,128)}, u32[]{:S(2)}) copy-start(f32[3,3,16,256]{3,2,1,0:T(8,128)} %param.15) | copy-start | bytes 442372
  8.4 58.1 %slice-start = ((f32[3,3,16,256]{3,2,1,0:T(8,128)}), f32[1,3,16,256]{3,2,1,0:T(8,128)S(1)}, s32[]{:S(2)}) async-start(f32[3,3,16,256]{3,2,1,0:T(8,128)} %param.15), calls=%async_computation | async-start | bytes 98304 | tf_op jit(solution)/shard_map/slice | solution.py:149
  8.4 58.1 %copy-start.21 = (f32[3,16,256]{2,1,0:T(8,128)S(1)}, f32[3,16,256]{2,1,0:T(8,128)}, u32[]{:S(2)}) copy-start(f32[3,16,256]{2,1,0:T(8,128)} %param.16) | copy-start | bytes 147460
  15.1 28.4 %collective-permute-start.4 = (f32[2,1,3,128]{3,0,2,1:T(2,128)S(1)}, f32[2,1,3,128]{3,0,2,1:T(2,128)S(1)}, u32[]{:S(2)}, u32[]{:S(2)}) collective-permute-start(f32[2,1,3,128]{3,0,2,1:T(2,128)S(1)} %get-tuple-element.196), channel_id=1, source_target_pairs={{0,16},{16,32},{32,48},{48,64},{64,80},{80,96},{96,112},{112,128},... | collective-permute-start | bytes 9224 | tf_op jit(solution)/shard_map/ppermute | solution.py:14
  20.5 23.1 %collective-permute-start.5 = (f32[2,1,3,128]{3,0,2,1:T(2,128)S(1)}, f32[2,1,3,128]{3,0,2,1:T(2,128)S(1)}, u32[]{:S(2)}, u32[]{:S(2)}) collective-permute-start(f32[2,1,3,128]{3,0,2,1:T(2,128)S(1)} %get-tuple-element.197), channel_id=1, source_target_pairs={{16,0},{32,16},{48,32},{64,48},{80,64},{96,80},{112,96},{128,112},... | collective-permute-start | bytes 9224 | tf_op jit(solution)/shard_map/ppermute | solution.py:15
  22.4 16.9 %collective-permute-start = (f32[3,1,256]{2,1,0:T(1,128)S(1)}, f32[3,1,256]{2,1,0:T(1,128)S(1)}, u32[]{:S(2)}, u32[]{:S(2)}) collective-permute-start(f32[3,1,256]{2,1,0:T(1,128)S(1)} %get-tuple-element.76), channel_id=1, source_target_pairs={{0,16},{16,32},{32,48},{48,64},{64,80},{80,96},{96,112},{112,128},... | collective-permute-start | bytes 9224 | tf_op jit(solution)/shard_map/ppermute | solution.py:14
  27.3 12.0 %collective-permute-start.1 = (f32[3,1,256]{2,1,0:T(1,128)S(1)}, f32[3,1,256]{2,1,0:T(1,128)S(1)}, u32[]{:S(2)}, u32[]{:S(2)}) collective-permute-start(f32[3,1,256]{2,1,0:T(1,128)S(1)} %get-tuple-element.77), channel_id=1, source_target_pairs={{16,0},{32,16},{48,32},{64,48},{80,64},{96,80},{112,96},{128,112},... | collective-permute-start | bytes 9224 | tf_op jit(solution)/shard_map/ppermute | solution.py:15
  38.6 61.5 %copy-start.25 = (pred[257]{0:T(512)(128)(4,1)}, pred[257]{0:T(512)(128)(4,1)S(1)}, u32[]{:S(2)}) copy-start(pred[257]{0:T(512)(128)(4,1)S(1)} %fusion.78) | copy-start | bytes 775
  39.4 9.4 %collective-permute-start.2 = (f32[3,66,1]{2,1,0:T(8,128)S(1)}, f32[3,66,1]{2,1,0:T(8,128)S(1)}, u32[]{:S(2)}, u32[]{:S(2)}) collective-permute-start(f32[3,66,1]{2,1,0:T(8,128)S(1)} %get-tuple-element.74), channel_id=1, source_target_pairs={{0,4},{4,8},{8,12},{1,5},{5,9},{9,13},{2,6},{6,10},{10,14},{3,7},{... | collective-permute-start | bytes 2384 | tf_op jit(solution)/shard_map/ppermute | solution.py:14
  42.2 6.6 %collective-permute-start.3 = (f32[3,66,1]{2,1,0:T(8,128)S(1)}, f32[3,66,1]{2,1,0:T(8,128)S(1)}, u32[]{:S(2)}, u32[]{:S(2)}) collective-permute-start(f32[3,66,1]{2,1,0:T(8,128)S(1)} %get-tuple-element.75), channel_id=1, source_target_pairs={{4,0},{8,4},{12,8},{5,1},{9,5},{13,9},{6,2},{10,6},{14,10},{7,3},{... | collective-permute-start | bytes 2384 | tf_op jit(solution)/shard_map/ppermute | solution.py:15
  43.5 5.6 %collective-permute-start.6 = (f32[2,5,1,128]{3,0,2,1:T(2,128)S(1)}, f32[2,5,1,128]{3,0,2,1:T(2,128)S(1)}, u32[]{:S(2)}, u32[]{:S(2)}) collective-permute-start(f32[2,5,1,128]{3,0,2,1:T(2,128)S(1)} %get-tuple-element.182), channel_id=1, source_target_pairs={{0,4},{4,8},{8,12},{1,5},{5,9},{9,13},{2,6},{6,10},{10,14},{3,7},{... | collective-permute-start | bytes 15368 | tf_op jit(solution)/shard_map/ppermute | solution.py:14
  47.5 4.4 %collective-permute-start.7 = (f32[2,5,1,128]{3,0,2,1:T(2,128)S(1)}, f32[2,5,1,128]{3,0,2,1:T(2,128)S(1)}, u32[]{:S(2)}, u32[]{:S(2)}) collective-permute-start(f32[2,5,1,128]{3,0,2,1:T(2,128)S(1)} %get-tuple-element.183), channel_id=1, source_target_pairs={{4,0},{8,4},{12,8},{5,1},{9,5},{13,9},{6,2},{10,6},{14,10},{7,3},{... | collective-permute-start | bytes 15368 | tf_op jit(solution)/shard_map/ppermute | solution.py:15
  66.7 9.2 %collective-permute-start.8 = (f32[13,1,256]{2,0,1:T(8,128)S(1)}, f32[13,1,256]{2,0,1:T(8,128)S(1)}, u32[]{:S(2)}, u32[]{:S(2)}) collective-permute-start(f32[13,1,256]{2,0,1:T(8,128)S(1)} %get-tuple-element.64), channel_id=1, source_target_pairs={{0,16},{16,32},{32,48},{48,64},{64,80},{80,96},{96,112},{112,128},... | collective-permute-start | bytes 39944 | tf_op jit(solution)/shard_map/ppermute | solution.py:14
  73.6 6.3 %collective-permute-start.9 = (f32[13,1,256]{2,0,1:T(8,128)S(1)}, f32[13,1,256]{2,0,1:T(8,128)S(1)}, u32[]{:S(2)}, u32[]{:S(2)}) collective-permute-start(f32[13,1,256]{2,0,1:T(8,128)S(1)} %get-tuple-element.65), channel_id=1, source_target_pairs={{16,0},{32,16},{48,32},{64,48},{80,64},{96,80},{112,96},{128,112},... | collective-permute-start | bytes 39944 | tf_op jit(solution)/shard_map/ppermute | solution.py:15
  80.1 4.8 %collective-permute-start.10 = (f32[13,18,1]{2,0,1:T(8,128)S(1)}, f32[13,18,1]{2,0,1:T(8,128)S(1)}, u32[]{:S(2)}, u32[]{:S(2)}) collective-permute-start(f32[13,18,1]{2,0,1:T(8,128)S(1)} %get-tuple-element.62), channel_id=1, source_target_pairs={{0,4},{4,8},{8,12},{1,5},{5,9},{9,13},{2,6},{6,10},{10,14},{3,7},{... | collective-permute-start | bytes 2816 | tf_op jit(solution)/shard_map/ppermute | solution.py:14
  82.8 5.9 %collective-permute-start.11 = (f32[13,18,1]{2,0,1:T(8,128)S(1)}, f32[13,18,1]{2,0,1:T(8,128)S(1)}, u32[]{:S(2)}, u32[]{:S(2)}) collective-permute-start(f32[13,18,1]{2,0,1:T(8,128)S(1)} %get-tuple-element.63), channel_id=1, source_target_pairs={{4,0},{8,4},{12,8},{5,1},{9,5},{13,9},{6,2},{10,6},{14,10},{7,3},{... | collective-permute-start | bytes 2816 | tf_op jit(solution)/shard_map/ppermute | solution.py:15
  89.2 5.9 %collective-permute-start.12 = (f32[4,1,18,258]{3,0,2,1:T(4,128)S(1)}, f32[4,1,18,258]{3,0,2,1:T(4,128)S(1)}, u32[]{:S(2)}, u32[]{:S(2)}) collective-permute-start(f32[4,1,18,258]{3,0,2,1:T(4,128)S(1)} %copy.245), channel_id=1, source_target_pairs={{0,1},{1,2},{2,3},{4,5},{5,6},{6,7},{8,9},{9,10},{10,11},{12,13},{... | collective-permute-start | bytes 222920 | tf_op jit(solution)/shard_map/ppermute | solution.py:14
  93.6 7.7 %collective-permute-start.13 = (f32[4,1,18,258]{3,0,2,1:T(4,128)S(1)}, f32[4,1,18,258]{3,0,2,1:T(4,128)S(1)}, u32[]{:S(2)}, u32[]{:S(2)}) collective-permute-start(f32[4,1,18,258]{3,0,2,1:T(4,128)S(1)} %copy.246), channel_id=1, source_target_pairs={{1,0},{2,1},{3,2},{5,4},{6,5},{7,6},{9,8},{10,9},{11,10},{13,12},{... | collective-permute-start | bytes 222920 | tf_op jit(solution)/shard_map/ppermute | solution.py:15
  98.9 10.8 %copy-start.11 = (f32[1,17,257]{2,0,1:T(1,128)S(1)}, f32[1,17,257]{2,0,1:T(1,128)}, u32[]{:S(2)}) copy-start(f32[1,17,257]{2,0,1:T(1,128)} %get-tuple-element.99) | copy-start | bytes 52432
  98.9 10.8 %copy-start.12 = (f32[1,17,257]{2,0,1:T(1,128)S(1)}, f32[1,17,257]{2,0,1:T(1,128)}, u32[]{:S(2)}) copy-start(f32[1,17,257]{2,0,1:T(1,128)} %get-tuple-element.100) | copy-start | bytes 52432
  98.9 10.8 %copy-start.13 = (f32[1,17,257]{2,0,1:T(1,128)S(1)}, f32[1,17,257]{2,0,1:T(1,128)}, u32[]{:S(2)}) copy-start(f32[1,17,257]{2,0,1:T(1,128)} %get-tuple-element.104) | copy-start | bytes 52432
  98.9 10.8 %copy-start.14 = (f32[1,17,257]{2,0,1:T(1,128)S(1)}, f32[1,17,257]{2,0,1:T(1,128)}, u32[]{:S(2)}) copy-start(f32[1,17,257]{2,0,1:T(1,128)} %get-tuple-element.153) | copy-start | bytes 52432
  98.9 10.8 %copy-start.15 = (f32[1,17,257]{2,0,1:T(1,128)S(1)}, f32[1,17,257]{2,0,1:T(1,128)}, u32[]{:S(2)}) copy-start(f32[1,17,257]{2,0,1:T(1,128)} %get-tuple-element.154) | copy-start | bytes 52432
  98.9 10.8 %copy-start.16 = (f32[1,17,257]{2,0,1:T(1,128)S(1)}, f32[1,17,257]{2,0,1:T(1,128)}, u32[]{:S(2)}) copy-start(f32[1,17,257]{2,0,1:T(1,128)} %get-tuple-element.155) | copy-start | bytes 52432
  100.0 15.1 %copy-start.6 = (f32[1,17,257]{2,0,1:T(1,128)}, f32[1,17,257]{2,0,1:T(1,128)S(1)}, u32[]{:S(2)}) copy-start(f32[1,17,257]{2,0,1:T(1,128)S(1)} %get-tuple-element.177) | copy-start | bytes 52432
  100.0 15.1 %copy-start.8 = (f32[1,17,257]{2,0,1:T(1,128)}, f32[1,17,257]{2,0,1:T(1,128)S(1)}, u32[]{:S(2)}) copy-start(f32[1,17,257]{2,0,1:T(1,128)S(1)} %get-tuple-element.178) | copy-start | bytes 52432
  100.0 15.1 %copy-start.9 = (f32[1,17,257]{2,0,1:T(1,128)}, f32[1,17,257]{2,0,1:T(1,128)S(1)}, u32[]{:S(2)}) copy-start(f32[1,17,257]{2,0,1:T(1,128)S(1)} %get-tuple-element.179) | copy-start | bytes 52432
  100.1 19.7 %copy-start.4 = (f32[1,17,257]{2,0,1:T(1,128)}, f32[1,17,257]{2,0,1:T(1,128)S(1)}, u32[]{:S(2)}) copy-start(f32[1,17,257]{2,0,1:T(1,128)S(1)} %get-tuple-element.167) | copy-start | bytes 52432
  115.9 7.2 %copy-start.7 = (f32[1,17,257]{2,0,1:T(1,128)S(1)}, f32[1,17,257]{2,0,1:T(1,128)}, u32[]{:S(2)}) copy-start(f32[1,17,257]{2,0,1:T(1,128)} %copy-done.6) | copy-start | bytes 52432
  120.8 6.1 %copy-start.5 = (f32[1,17,257]{2,0,1:T(1,128)S(1)}, f32[1,17,257]{2,0,1:T(1,128)}, u32[]{:S(2)}) copy-start(f32[1,17,257]{2,0,1:T(1,128)} %copy-done.4) | copy-start | bytes 52432
  124.5 10.9 %copy-start.17 = (pred[16,256]{1,0:T(8,128)(4,1)S(1)}, pred[16,256]{1,0:T(8,128)(4,1)}, u32[]{:S(2)}) copy-start(pred[16,256]{1,0:T(8,128)(4,1)} %get-tuple-element.192) | copy-start | bytes 12292
  124.5 10.9 %copy-start.18 = (pred[16,256]{1,0:T(8,128)(4,1)S(1)}, pred[16,256]{1,0:T(8,128)(4,1)}, u32[]{:S(2)}) copy-start(pred[16,256]{1,0:T(8,128)(4,1)} %get-tuple-element.193) | copy-start | bytes 12292
  124.5 10.9 %copy-start.19 = (pred[16,256]{1,0:T(8,128)(4,1)S(1)}, pred[16,256]{1,0:T(8,128)(4,1)}, u32[]{:S(2)}) copy-start(pred[16,256]{1,0:T(8,128)(4,1)} %get-tuple-element.194) | copy-start | bytes 12292
  124.6 10.9 %copy-start.20 = (pred[16,256]{1,0:T(8,128)(4,1)S(1)}, pred[16,256]{1,0:T(8,128)(4,1)}, u32[]{:S(2)}) copy-start(pred[16,256]{1,0:T(8,128)(4,1)} %get-tuple-element.195) | copy-start | bytes 12292
  129.8 30.5 %copy-start.3 = (f32[64,256]{1,0:T(8,128)S(1)}, f32[64,256]{1,0:T(8,128)}, u32[]{:S(2)}) copy-start(f32[64,256]{1,0:T(8,128)} %param.13) | copy-start | bytes 196612
  154.4 8.9 %collective-permute-start.14 = (f32[2,1,3,128]{3,0,2,1:T(2,128)S(1)}, f32[2,1,3,128]{3,0,2,1:T(2,128)S(1)}, u32[]{:S(2)}, u32[]{:S(2)}) collective-permute-start(f32[2,1,3,128]{3,0,2,1:T(2,128)S(1)} %get-tuple-element.185), channel_id=1, source_target_pairs={{0,16},{16,32},{32,48},{48,64},{64,80},{80,96},{96,112},{112,128},... | collective-permute-start | bytes 9224 | tf_op jit(solution)/shard_map/ppermute | solution.py:14
  161.4 6.1 %collective-permute-start.15 = (f32[2,1,3,128]{3,0,2,1:T(2,128)S(1)}, f32[2,1,3,128]{3,0,2,1:T(2,128)S(1)}, u32[]{:S(2)}, u32[]{:S(2)}) collective-permute-start(f32[2,1,3,128]{3,0,2,1:T(2,128)S(1)} %get-tuple-element.184), channel_id=1, source_target_pairs={{16,0},{32,16},{48,32},{64,48},{80,64},{96,80},{112,96},{128,112},... | collective-permute-start | bytes 9224 | tf_op jit(solution)/shard_map/ppermute | solution.py:15
  167.5 6.3 %collective-permute-start.16 = (f32[2,5,1,128]{3,0,2,1:T(2,128)S(1)}, f32[2,5,1,128]{3,0,2,1:T(2,128)S(1)}, u32[]{:S(2)}, u32[]{:S(2)}) collective-permute-start(f32[2,5,1,128]{3,0,2,1:T(2,128)S(1)} %get-tuple-element.180), channel_id=1, source_target_pairs={{0,4},{4,8},{8,12},{1,5},{5,9},{9,13},{2,6},{6,10},{10,14},{3,7},{... | collective-permute-start | bytes 15368 | tf_op jit(solution)/shard_map/ppermute | solution.py:14
  170.8 4.4 %collective-permute-start.17 = (f32[2,5,1,128]{3,0,2,1:T(2,128)S(1)}, f32[2,5,1,128]{3,0,2,1:T(2,128)S(1)}, u32[]{:S(2)}, u32[]{:S(2)}) collective-permute-start(f32[2,5,1,128]{3,0,2,1:T(2,128)S(1)} %get-tuple-element.181), channel_id=1, source_target_pairs={{4,0},{8,4},{12,8},{5,1},{9,5},{13,9},{6,2},{10,6},{14,10},{7,3},{... | collective-permute-start | bytes 15368 | tf_op jit(solution)/shard_map/ppermute | solution.py:15
where the time goes:
time: 203 us; the launch traced here: 201 us
  local copies, waits for them, and re-layouts  62.5 us (31%)
  starting transfers between devices  53.3 us (26%)
  other arithmetic  51.7 us (25%)
  waiting for transfers between devices  16.8 us (8%)
  blocking collectives  9.58 us (5%)
  matrix products  5.27 us (3%)
    ppermute x9, starting transfers between devices, with_halo(): before = lax.ppermute(last, axis, up)  39 us
    ppermute x9, waiting for transfers between devices, with_halo(): after = lax.ppermute(initial, axis, down)  16.2 us
    ppermute x9, starting transfers between devices, with_halo(): after = lax.ppermute(initial, axis, down)  14.3 us
    scatter-add x1, other arithmetic, per_device(): node_force = jnp.zeros((2, row_count * col_count + 1), jnp.float32).at[:,...  14 us
    another operation x8, local copies, waits for them, and re-layouts, triangle(): jnp.stack([plane[comp] for group in (lows, ups) for comp in range(3) for...  11.7 us
    unnamed x71, local copies, waits for them, and re-layouts  10.8 us
    scatter-add x1, other arithmetic, per_device(): placed = jnp.zeros((2, column_count + 1), jnp.float32).at[:, target].add(...  10.6 us
    psum x1, blocking collectives, per_device(): depth_total = lax.psum(bucket, 'layer')  9.58 us
  transfers between devices with their start and end apart: 18, of which 6 were waited for; matrix products, arithmetic and copies ran while one was open for 10% of the time, Pallas kernels for 0%

commit v1 on v0

--- a/solution.py
+++ b/solution.py
@@ -2,6 +2,7 @@
 import jax.numpy as jnp
 from jax import lax
 from jax.sharding import PartitionSpec as P
+from jax.lax import all_gather
 
 
 def with_halo(array, sides, width):
@@ -192,7 +193,7 @@
     stokes_residual = jnp.stack(owned, axis=1) - body_force
     depth_sum = jnp.sum(stokes_residual[:2], axis=1).reshape(2, column_count)
     bucket = jnp.where(col_live[None], depth_sum[:, jnp.maximum(columns, 0)], 0.0)
-    depth_total = lax.psum(bucket, "layer")
+    depth_total = all_gather(bucket, "layer").sum(axis=0)
     grid_back = depth_total.reshape(2, 3, 3, slot_count)
     extended_back = with_halo(grid_back, (("mx", 1), ("my", 2)), 1)
     at_owner = extended_back[:, 0::2, 0::2].reshape(2, 9, slot_count)

time: 203 us -> 199 us (0.980)
  local copies, waits for them, and re-layouts: 62.5 us -> 59.4 us
    all_gather x0 -> x1, blocking collectives: none -> 10.2 us  [per_device(): depth_total = all_gather(bucket, 'layer').sum(axis=0)]
    psum x1 -> x0, blocking collectives: 9.58 us -> none  [per_device(): depth_total = lax.psum(bucket, 'layer')]
    unnamed x71 -> x67, local copies, waits for them, and re-layouts: 10.8 us -> 8.49 us
    slice x15 -> x10, local copies, waits for them, and re-layouts: 5.54 us -> 4.38 us  [triangle(): plane[comp]]
where the time goes in v1:
time: 199 us; the launch traced here: 197 us
  local copies, waits for them, and re-layouts  59.4 us (30%)
  starting transfers between devices  54.2 us (27%)
  other arithmetic  49.7 us (25%)
  waiting for transfers between devices  15.8 us (8%)
  blocking collectives  10.2 us (5%)
  matrix products  6.07 us (3%)
    ppermute x9, starting transfers between devices, with_halo(): before = lax.ppermute(last, axis, up)  39.9 us
    ppermute x9, waiting for transfers between devices, with_halo(): after = lax.ppermute(initial, axis, down)  15.2 us
    ppermute x9, starting transfers between devices, with_halo(): after = lax.ppermute(initial, axis, down)  14.3 us
    scatter-add x1, other arithmetic, per_device(): node_force = jnp.zeros((2, row_count * col_count + 1), jnp.float32).at[:,...  14 us
    another operation x8, local copies, waits for them, and re-layouts, triangle(): jnp.stack([plane[comp] for group in (lows, ups) for comp in range(3) for...  12.4 us
    scatter-add x1, other arithmetic, per_device(): placed = jnp.zeros((2, column_count + 1), jnp.float32).at[:, target].add(...  10.6 us
    all_gather x1, blocking collectives, per_device(): depth_total = all_gather(bucket, 'layer').sum(axis=0)  10.2 us
    scatter-add x1, other arithmetic, per_device(): jnp.zeros((column_count + 1,), jnp.float32).at[target].add(1.0)  8.69 us
  transfers between devices with their start and end apart: 18, of which 6 were waited for; matrix products, arithmetic and copies ran while one was open for 10% of the time, Pallas kernels for 0%

profile of v1, /device:TPU:97, one launch (start us, length us, event | category | flops | bytes accessed | tf_op | source)
XLA Modules:
  0.0 197.3 jit_solution(15354366289654764724)
XLA Ops:
  0.7 0.8 maximum_reduce_fusion.1
  1.5 0.7 compare_reduce_fusion
  2.2 5.5 %copy.172 = f32[2,64,256]{0,2,1:T(8,128)} copy(f32[2,64,256]{2,1,0:T(8,128)} %param.11) | data formatting | bytes 262144 | tf_op args[0]
  7.8 5.9 %gather_fusion = f32[1152,2]{1,0:T(8,128)S(1)} fusion(f32[2,16384]{0,1:T(8,128)} %bitcast.291, s32[2048]{0:T(1024)S(1)} %pad_clamp_fusion.1), kind=kCustom, calls=%fused_computation | custom fusion | bytes 23040 | tf_op jit(solution)/shard_map/gather | solution.py:127
  13.9 5.3 %collective-permute-start.4 = (f32[2,1,3,128]{3,0,2,1:T(2,128)S(1)}, f32[2,1,3,128]{3,0,2,1:T(2,128)S(1)}, u32[]{:S(2)}, u32[]{:S(2)}) collective-permute-start(f32[2,1,3,128]{3,0,2,1:T(2,128)S(1)} %get-tuple-element.196), channel_id=1, source_target_pairs={{0,16},{16,32},{32,48},{48,64},{64,80},{80,96},{96,112},{112,128},... | collective-permute-start | bytes 9224 | tf_op jit(solution)/shard_map/ppermute | solution.py:15
  19.2 1.9 collective-permute-start.5
  21.2 4.9 %collective-permute-start = (f32[3,1,256]{2,1,0:T(1,128)S(1)}, f32[3,1,256]{2,1,0:T(1,128)S(1)}, u32[]{:S(2)}, u32[]{:S(2)}) collective-permute-start(f32[3,1,256]{2,1,0:T(1,128)S(1)} %get-tuple-element.76), channel_id=1, source_target_pairs={{0,16},{16,32},{32,48},{48,64},{64,80},{80,96},{96,112},{112,128},... | collective-permute-start | bytes 9224 | tf_op jit(solution)/shard_map/ppermute | solution.py:15
  26.0 1.9 collective-permute-start.1
  28.7 8.7 %scatter_custom_fusion = f32[4097]{0:T(1024)S(1)} fusion(s32[1152]{0:T(1024)S(1)} %fusion.75, f32[1152]{0:T(1024)S(1)} %broadcast.313, f32[]{:T(128)} %constant.32.clone.1), kind=kCustom, calls=%fused_computation.251 | custom fusion | flops 1152 | bytes 16392 | tf_op jit(solution)/shard_map/scatter-add | solution.py:144
  38.8 2.8 %collective-permute-start.2 = (f32[3,66,1]{2,1,0:T(8,128)S(1)}, f32[3,66,1]{2,1,0:T(8,128)S(1)}, u32[]{:S(2)}, u32[]{:S(2)}) collective-permute-start(f32[3,66,1]{2,1,0:T(8,128)S(1)} %get-tuple-element.74), channel_id=1, source_target_pairs={{0,4},{4,8},{8,12},{1,5},{5,9},{9,13},{2,6},{6,10},{10,14},{3,7},{... | collective-permute-start | bytes 2384 | tf_op jit(solution)/shard_map/ppermute | solution.py:15
  41.6 1.3 collective-permute-start.3
  42.9 4.0 %collective-permute-start.6 = (f32[2,5,1,128]{3,0,2,1:T(2,128)S(1)}, f32[2,5,1,128]{3,0,2,1:T(2,128)S(1)}, u32[]{:S(2)}, u32[]{:S(2)}) collective-permute-start(f32[2,5,1,128]{3,0,2,1:T(2,128)S(1)} %get-tuple-element.182), channel_id=1, source_target_pairs={{0,4},{4,8},{8,12},{1,5},{5,9},{9,13},{2,6},{6,10},{10,14},{3,7},{... | collective-permute-start | bytes 15368 | tf_op jit(solution)/shard_map/ppermute | solution.py:15
  46.9 1.3 collective-permute-start.7
  48.5 2.8 %collective-permute-done.7 = f32[2,5,1,128]{3,0,2,1:T(2,128)S(1)} collective-permute-done((f32[2,5,1,128]{3,0,2,1:T(2,128)S(1)}, f32[2,5,1,128]{3,0,2,1:T(2,128)S(1)}, u32[]{:S(2)}, u32[]{:S(2)}) %collective-permute-start.7) | collective-permute-done | bytes 5152 | tf_op jit(solution)/shard_map/ppermute | solution.py:16
  51.6 10.6 %scatter_custom_fusion.1 = f32[2,4097]{0,1:T(8,128)S(1)} fusion(s32[1152]{0:T(1024)S(1)} %fusion.75, f32[1152,2]{1,0:T(8,128)S(1)} %copy.174, f32[]{:T(128)} %constant.32.clone.1), kind=kCustom, calls=%fused_computation.23 | custom fusion | flops 2304 | bytes 32780 | tf_op jit(solution)/shard_map/scatter-add | solution.py:142
  62.2 1.5 slice.1284
  63.6 2.2 %copy.175 = f32[2,16,256]{2,1,0:T(8,128)S(1)} copy(f32[2,16,256]{0,2,1:T(8,128)} %bitcast.292) | data formatting | bytes 65536 | tf_op jit(solution)/shard_map/jit(_where)/broadcast_in_dim | solution.py:145
  66.1 7.0 %collective-permute-start.8 = (f32[13,1,256]{2,0,1:T(8,128)S(1)}, f32[13,1,256]{2,0,1:T(8,128)S(1)}, u32[]{:S(2)}, u32[]{:S(2)}) collective-permute-start(f32[13,1,256]{2,0,1:T(8,128)S(1)} %get-tuple-element.64), channel_id=1, source_target_pairs={{0,16},{16,32},{32,48},{48,64},{64,80},{80,96},{96,112},{112,128},... | collective-permute-start | bytes 39944 | tf_op jit(solution)/shard_map/ppermute | solution.py:15
  73.0 1.9 collective-permute-start.9
  75.2 4.1 %collective-permute-done.9 = f32[13,1,256]{2,0,1:T(8,128)S(1)} collective-permute-done((f32[13,1,256]{2,0,1:T(8,128)S(1)}, f32[13,1,256]{2,0,1:T(8,128)S(1)}, u32[]{:S(2)}, u32[]{:S(2)}) %collective-permute-start.9) | collective-permute-done | bytes 13344 | tf_op jit(solution)/shard_map/ppermute | solution.py:16
  79.4 2.7 %collective-permute-start.10 = (f32[13,18,1]{2,0,1:T(8,128)S(1)}, f32[13,18,1]{2,0,1:T(8,128)S(1)}, u32[]{:S(2)}, u32[]{:S(2)}) collective-permute-start(f32[13,18,1]{2,0,1:T(8,128)S(1)} %get-tuple-element.62), channel_id=1, source_target_pairs={{0,4},{4,8},{8,12},{1,5},{5,9},{9,13},{2,6},{6,10},{10,14},{3,7},{... | collective-permute-start | bytes 2816 | tf_op jit(solution)/shard_map/ppermute | solution.py:15
  82.2 1.3 collective-permute-start.11
  84.3 3.8 %collective-permute-done.11 = f32[13,18,1]{2,0,1:T(8,128)S(1)} collective-permute-done((f32[13,18,1]{2,0,1:T(8,128)S(1)}, f32[13,18,1]{2,0,1:T(8,128)S(1)}, u32[]{:S(2)}, u32[]{:S(2)}) %collective-permute-start.11) | collective-permute-done | bytes 968 | tf_op jit(solution)/shard_map/ppermute | solution.py:16
  88.6 3.1 %collective-permute-start.12 = (f32[4,1,18,258]{3,0,2,1:T(4,128)S(1)}, f32[4,1,18,258]{3,0,2,1:T(4,128)S(1)}, u32[]{:S(2)}, u32[]{:S(2)}) collective-permute-start(f32[4,1,18,258]{3,0,2,1:T(4,128)S(1)} %copy.245), channel_id=1, source_target_pairs={{0,1},{1,2},{2,3},{4,5},{5,6},{6,7},{8,9},{9,10},{10,11},{12,13},{... | collective-permute-start | bytes 222920 | tf_op jit(solution)/shard_map/ppermute | solution.py:15
  93.1 1.5 collective-permute-start.13
  95.1 1.1 fusion.87
  96.2 0.8 fusion.92
  98.2 1.2 and_select_fusion.3
  99.8 1.9 and_select_fusion.1
  101.6 0.8 fusion.96
  102.4 1.1 fusion.89
  103.6 2.3 %stack.48 = f32[18,17,257]{2,0,1:T(8,128)S(1)} concatenate(f32[1,17,257]{2,0,1:T(1,128)} %get-tuple-element.106, f32[1,17,257]{2,0,1:T(1,128)} %get-tuple-element.105, f32[1,17,257]{2,0,1:T(1,128)} %get-tuple-element.152, f32[1,17,257]{2,0,1:T(1,128)} %get-tuple-element.103, f32[1,17,257]{2,0,1:T(1,128)} %get-tuple-element.102, f32[1,17,257]{2,0,1:T(1,128)} %get-tuple-element.151, ...), dimensions={0} | concatenate | bytes 629136 | tf_op jit(solution)/shard_map/stack | solution.py:47
  106.6 0.7 slice_bitcast_fusion.35
  107.4 0.8 stack.49
  109.7 0.8 stack.50
  111.3 0.7 slice_bitcast_fusion.33
  112.0 0.8 stack.51
  113.6 0.7 slice_bitcast_fusion.32
  114.4 0.7 slice_bitcast_fusion.23
  115.2 0.7 slice_bitcast_fusion.22
  116.0 1.0 stack.53
  117.9 0.7 slice_bitcast_fusion.21
  118.6 1.5 stack.54
  121.6 1.4 copy_bitcast_fusion.1
  123.0 3.0 %stack.56 = f32[18,17,257]{2,0,1:T(8,128)S(1)} concatenate(f32[1,17,257]{2,0,1:T(1,128)} %copy-done.8, f32[1,17,257]{2,0,1:T(1,128)S(1)} %copy-done.7, f32[1,17,257]{2,0,1:T(1,128)S(1)} %get-tuple-element.167, f32[1,17,257]{2,0,1:T(1,128)S(1)} %copy-done.5, f32[1,17,257]{2,0,1:T(1,128)S(1)} %get-tuple-element.139, f32[1,17,257]{2,0,1:T(1,128)S(1)} %get-tuple-element.166, ...), dimensions={0} | concatenate | bytes 629136 | tf_op jit(solution)/shard_map/stack | solution.py:47
  126.0 1.5 fusion.3
  129.0 2.3 %stack.57 = f32[18,17,257]{2,0,1:T(8,128)S(1)} concatenate(f32[1,17,257]{2,0,1:T(1,128)S(1)} %get-tuple-element.204, f32[1,17,257]{2,0,1:T(1,128)S(1)} %get-tuple-element.137, f32[1,17,257]{2,0,1:T(1,128)S(1)} %get-tuple-element.118, f32[1,17,257]{2,0,1:T(1,128)S(1)} %get-tuple-element.205, f32[1,17,257]{2,0,1:T(1,128)S(1)} %get-tuple-element.117, ...), dimensions={0} | concatenate | bytes 629136 | tf_op jit(solution)/shard_map/stack | solution.py:47
  132.3 1.3 fusion.39
  133.7 1.4 fusion.47
  135.0 1.1 fusion.27
  136.1 0.9 maximum_subtract_fusion
  137.7 2.4 %gather_fusion.1 = f32[1152,2]{1,0:T(8,128)S(1)} fusion(f32[2,4096]{0,1:T(8,128)S(1)} %bitcast.299, s32[2048]{0:T(1024)S(1)} %copy-done.23), kind=kCustom, calls=%fused_computation.1 | custom fusion | bytes 23040 | tf_op jit(solution)/shard_map/gather | solution.py:195
  140.4 10.2 %all_gather.4 = f32[4,2,9,128]{3,1,2,0:T(2,128)S(1)} all-gather(f32[1,2,9,128]{3,1,2,0:T(2,128)S(1)} %bitcast_select_fusion), channel_id=1, replica_groups=mesh['mx'=32,'my'=4,'layer'=4] {'layer'}, dimensions={0}, use_global_device_ids=true | all-gather | bytes 46080 | tf_op jit(solution)/shard_map/all_gather | solution.py:196
  150.7 6.8 %collective-permute-start.14 = (f32[2,1,3,128]{3,0,2,1:T(2,128)S(1)}, f32[2,1,3,128]{3,0,2,1:T(2,128)S(1)}, u32[]{:S(2)}, u32[]{:S(2)}) collective-permute-start(f32[2,1,3,128]{3,0,2,1:T(2,128)S(1)} %get-tuple-element.184), channel_id=1, source_target_pairs={{0,16},{16,32},{32,48},{48,64},{64,80},{80,96},{96,112},{112,128},... | collective-permute-start | bytes 9224 | tf_op jit(solution)/shard_map/ppermute | solution.py:15
  157.5 1.9 collective-permute-start.15
  159.5 1.0 fusion.15
  160.5 3.2 %collective-permute-done.15 = f32[2,1,3,128]{3,0,2,1:T(2,128)S(1)} collective-permute-done((f32[2,1,3,128]{3,0,2,1:T(2,128)S(1)}, f32[2,1,3,128]{3,0,2,1:T(2,128)S(1)}, u32[]{:S(2)}, u32[]{:S(2)}) %collective-permute-start.15) | collective-permute-done | bytes 3104 | tf_op jit(solution)/shard_map/ppermute | solution.py:16
  163.7 3.3 %collective-permute-start.16 = (f32[2,5,1,128]{3,0,2,1:T(2,128)S(1)}, f32[2,5,1,128]{3,0,2,1:T(2,128)S(1)}, u32[]{:S(2)}, u32[]{:S(2)}) collective-permute-start(f32[2,5,1,128]{3,0,2,1:T(2,128)S(1)} %get-tuple-element.180), channel_id=1, source_target_pairs={{0,4},{4,8},{8,12},{1,5},{5,9},{9,13},{2,6},{6,10},{10,14},{3,7},{... | collective-permute-start | bytes 15368 | tf_op jit(solution)/shard_map/ppermute | solution.py:15
  167.0 1.3 collective-permute-start.17
  168.3 1.0 fusion.21
  170.0 1.4 collective-permute-done.17
  171.6 14.0 %scatter_custom_fusion.2 = f32[2,16385]{0,1:T(8,128)} fusion(s32[1152]{0:T(1024)} %fusion.74, f32[1152,2]{1,0:T(8,128)S(1)} %copy.231, f32[]{:T(128)} %constant.32.clone.1), kind=kCustom, calls=%fused_computation.5 | custom fusion | flops 2304 | bytes 131592 | tf_op jit(solution)/shard_map/scatter-add | solution.py:204
  185.6 5.7 %slice.1541 = f32[2,16384]{0,1:T(8,128)} slice(f32[2,16385]{0,1:T(8,128)} %scatter_custom_fusion.2), slice={[0:2], [0:16384]} | slice | bytes 262144 | tf_op jit(solution)/shard_map/slice | solution.py:206
  191.4 5.2 %copy.232 = f32[2,64,256]{2,1,0:T(8,128)S(1)} copy(f32[2,64,256]{0,2,1:T(8,128)} %bitcast.278) | data formatting | bytes 262144 | tf_op jit(solution)/shard_map/reshape | solution.py:206
  (173 shorter events, 19.3 us)
Async XLA Ops:
  0.6 105.2 %copy-start = (f32[18,18]{1,0:T(8,128)S(1)}, f32[18,18]{1,0:T(8,128)}, u32[]{:S(2)}) copy-start(f32[18,18]{1,0:T(8,128)} %param.19) | copy-start | bytes 3892
  0.6 27.4 %copy-start.22 = (s32[1,9,128]{2,0,1:T(1,128)S(1)}, s32[1,9,128]{2,0,1:T(1,128)}, u32[]{:S(2)}) copy-start(s32[1,9,128]{2,0,1:T(1,128)} %param.21) | copy-start | bytes 13828
  0.7 20.5 %copy-start.1 = (f32[2,64,256]{2,1,0:T(8,128)S(1)}, f32[2,64,256]{2,1,0:T(8,128)}, u32[]{:S(2)}) copy-start(f32[2,64,256]{2,1,0:T(8,128)} %param.11) | copy-start | bytes 393220
  0.7 20.5 %copy-start.2 = (f32[64,256]{1,0:T(8,128)S(1)}, f32[64,256]{1,0:T(8,128)}, u32[]{:S(2)}) copy-start(f32[64,256]{1,0:T(8,128)} %param.12) | copy-start | bytes 196612
  0.7 27.3 %copy-start.21 = (s32[1,9,128]{2,0,1:T(1,128)S(1)}, s32[1,9,128]{2,0,1:T(1,128)}, u32[]{:S(2)}) copy-start(s32[1,9,128]{2,0,1:T(1,128)} %param.20) | copy-start | bytes 13828
  0.7 37.4 %copy-start.24 = (s32[16,256]{1,0:T(8,128)S(1)}, s32[16,256]{1,0:T(8,128)}, u32[]{:S(2)}) copy-start(s32[16,256]{1,0:T(8,128)} %param.18) | copy-start | bytes 49156
  7.7 58.1 %copy-start.10 = (f32[3,3,16,256]{3,2,1,0:T(8,128)S(1)}, f32[3,3,16,256]{3,2,1,0:T(8,128)}, u32[]{:S(2)}) copy-start(f32[3,3,16,256]{3,2,1,0:T(8,128)} %param.15) | copy-start | bytes 442372
  7.8 58.1 %slice-start = ((f32[3,3,16,256]{3,2,1,0:T(8,128)}), f32[1,3,16,256]{3,2,1,0:T(8,128)S(1)}, s32[]{:S(2)}) async-start(f32[3,3,16,256]{3,2,1,0:T(8,128)} %param.15), calls=%async_computation | async-start | bytes 98304 | tf_op jit(solution)/shard_map/slice | solution.py:150
  7.8 58.1 %copy-start.20 = (f32[3,16,256]{2,1,0:T(8,128)S(1)}, f32[3,16,256]{2,1,0:T(8,128)}, u32[]{:S(2)}) copy-start(f32[3,16,256]{2,1,0:T(8,128)} %param.16) | copy-start | bytes 147460
  13.9 29.0 %collective-permute-start.4 = (f32[2,1,3,128]{3,0,2,1:T(2,128)S(1)}, f32[2,1,3,128]{3,0,2,1:T(2,128)S(1)}, u32[]{:S(2)}, u32[]{:S(2)}) collective-permute-start(f32[2,1,3,128]{3,0,2,1:T(2,128)S(1)} %get-tuple-element.196), channel_id=1, source_target_pairs={{0,16},{16,32},{32,48},{48,64},{64,80},{80,96},{96,112},{112,128},... | collective-permute-start | bytes 9224 | tf_op jit(solution)/shard_map/ppermute | solution.py:15
  19.2 23.7 %collective-permute-start.5 = (f32[2,1,3,128]{3,0,2,1:T(2,128)S(1)}, f32[2,1,3,128]{3,0,2,1:T(2,128)S(1)}, u32[]{:S(2)}, u32[]{:S(2)}) collective-permute-start(f32[2,1,3,128]{3,0,2,1:T(2,128)S(1)} %get-tuple-element.197), channel_id=1, source_target_pairs={{16,0},{32,16},{48,32},{64,48},{80,64},{96,80},{112,96},{128,112},... | collective-permute-start | bytes 9224 | tf_op jit(solution)/shard_map/ppermute | solution.py:16
  21.2 17.5 %collective-permute-start = (f32[3,1,256]{2,1,0:T(1,128)S(1)}, f32[3,1,256]{2,1,0:T(1,128)S(1)}, u32[]{:S(2)}, u32[]{:S(2)}) collective-permute-start(f32[3,1,256]{2,1,0:T(1,128)S(1)} %get-tuple-element.76), channel_id=1, source_target_pairs={{0,16},{16,32},{32,48},{48,64},{64,80},{80,96},{96,112},{112,128},... | collective-permute-start | bytes 9224 | tf_op jit(solution)/shard_map/ppermute | solution.py:15
  26.0 12.6 %collective-permute-start.1 = (f32[3,1,256]{2,1,0:T(1,128)S(1)}, f32[3,1,256]{2,1,0:T(1,128)S(1)}, u32[]{:S(2)}, u32[]{:S(2)}) collective-permute-start(f32[3,1,256]{2,1,0:T(1,128)S(1)} %get-tuple-element.77), channel_id=1, source_target_pairs={{16,0},{32,16},{48,32},{64,48},{80,64},{96,80},{112,96},{128,112},... | collective-permute-start | bytes 9224 | tf_op jit(solution)/shard_map/ppermute | solution.py:16
  38.0 60.1 %copy-start.25 = (pred[257]{0:T(512)(128)(4,1)}, pred[257]{0:T(512)(128)(4,1)S(1)}, u32[]{:S(2)}) copy-start(pred[257]{0:T(512)(128)(4,1)S(1)} %fusion.78) | copy-start | bytes 775
  38.8 9.4 %collective-permute-start.2 = (f32[3,66,1]{2,1,0:T(8,128)S(1)}, f32[3,66,1]{2,1,0:T(8,128)S(1)}, u32[]{:S(2)}, u32[]{:S(2)}) collective-permute-start(f32[3,66,1]{2,1,0:T(8,128)S(1)} %get-tuple-element.74), channel_id=1, source_target_pairs={{0,4},{4,8},{8,12},{1,5},{5,9},{9,13},{2,6},{6,10},{10,14},{3,7},{... | collective-permute-start | bytes 2384 | tf_op jit(solution)/shard_map/ppermute | solution.py:15
  41.6 6.6 %collective-permute-start.3 = (f32[3,66,1]{2,1,0:T(8,128)S(1)}, f32[3,66,1]{2,1,0:T(8,128)S(1)}, u32[]{:S(2)}, u32[]{:S(2)}) collective-permute-start(f32[3,66,1]{2,1,0:T(8,128)S(1)} %get-tuple-element.75), channel_id=1, source_target_pairs={{4,0},{8,4},{12,8},{5,1},{9,5},{13,9},{6,2},{10,6},{14,10},{7,3},{... | collective-permute-start | bytes 2384 | tf_op jit(solution)/shard_map/ppermute | solution.py:16
  42.9 5.6 %collective-permute-start.6 = (f32[2,5,1,128]{3,0,2,1:T(2,128)S(1)}, f32[2,5,1,128]{3,0,2,1:T(2,128)S(1)}, u32[]{:S(2)}, u32[]{:S(2)}) collective-permute-start(f32[2,5,1,128]{3,0,2,1:T(2,128)S(1)} %get-tuple-element.182), channel_id=1, source_target_pairs={{0,4},{4,8},{8,12},{1,5},{5,9},{9,13},{2,6},{6,10},{10,14},{3,7},{... | collective-permute-start | bytes 15368 | tf_op jit(solution)/shard_map/ppermute | solution.py:15
  46.9 4.4 %collective-permute-start.7 = (f32[2,5,1,128]{3,0,2,1:T(2,128)S(1)}, f32[2,5,1,128]{3,0,2,1:T(2,128)S(1)}, u32[]{:S(2)}, u32[]{:S(2)}) collective-permute-start(f32[2,5,1,128]{3,0,2,1:T(2,128)S(1)} %get-tuple-element.183), channel_id=1, source_target_pairs={{4,0},{8,4},{12,8},{5,1},{9,5},{13,9},{6,2},{10,6},{14,10},{7,3},{... | collective-permute-start | bytes 15368 | tf_op jit(solution)/shard_map/ppermute | solution.py:16
  66.1 9.2 %collective-permute-start.8 = (f32[13,1,256]{2,0,1:T(8,128)S(1)}, f32[13,1,256]{2,0,1:T(8,128)S(1)}, u32[]{:S(2)}, u32[]{:S(2)}) collective-permute-start(f32[13,1,256]{2,0,1:T(8,128)S(1)} %get-tuple-element.64), channel_id=1, source_target_pairs={{0,16},{16,32},{32,48},{48,64},{64,80},{80,96},{96,112},{112,128},... | collective-permute-start | bytes 39944 | tf_op jit(solution)/shard_map/ppermute | solution.py:15
  73.0 6.3 %collective-permute-start.9 = (f32[13,1,256]{2,0,1:T(8,128)S(1)}, f32[13,1,256]{2,0,1:T(8,128)S(1)}, u32[]{:S(2)}, u32[]{:S(2)}) collective-permute-start(f32[13,1,256]{2,0,1:T(8,128)S(1)} %get-tuple-element.65), channel_id=1, source_target_pairs={{16,0},{32,16},{48,32},{64,48},{80,64},{96,80},{112,96},{128,112},... | collective-permute-start | bytes 39944 | tf_op jit(solution)/shard_map/ppermute | solution.py:16
  79.4 4.8 %collective-permute-start.10 = (f32[13,18,1]{2,0,1:T(8,128)S(1)}, f32[13,18,1]{2,0,1:T(8,128)S(1)}, u32[]{:S(2)}, u32[]{:S(2)}) collective-permute-start(f32[13,18,1]{2,0,1:T(8,128)S(1)} %get-tuple-element.62), channel_id=1, source_target_pairs={{0,4},{4,8},{8,12},{1,5},{5,9},{9,13},{2,6},{6,10},{10,14},{3,7},{... | collective-permute-start | bytes 2816 | tf_op jit(solution)/shard_map/ppermute | solution.py:15
  82.2 5.9 %collective-permute-start.11 = (f32[13,18,1]{2,0,1:T(8,128)S(1)}, f32[13,18,1]{2,0,1:T(8,128)S(1)}, u32[]{:S(2)}, u32[]{:S(2)}) collective-permute-start(f32[13,18,1]{2,0,1:T(8,128)S(1)} %get-tuple-element.63), channel_id=1, source_target_pairs={{4,0},{8,4},{12,8},{5,1},{9,5},{13,9},{6,2},{10,6},{14,10},{7,3},{... | collective-permute-start | bytes 2816 | tf_op jit(solution)/shard_map/ppermute | solution.py:16
  88.6 5.9 %collective-permute-start.12 = (f32[4,1,18,258]{3,0,2,1:T(4,128)S(1)}, f32[4,1,18,258]{3,0,2,1:T(4,128)S(1)}, u32[]{:S(2)}, u32[]{:S(2)}) collective-permute-start(f32[4,1,18,258]{3,0,2,1:T(4,128)S(1)} %copy.245), channel_id=1, source_target_pairs={{0,1},{1,2},{2,3},{4,5},{5,6},{6,7},{8,9},{9,10},{10,11},{12,13},{... | collective-permute-start | bytes 222920 | tf_op jit(solution)/shard_map/ppermute | solution.py:15
  92.3 19.7 %copy-start.9 = (f32[1,17,257]{2,0,1:T(1,128)}, f32[1,17,257]{2,0,1:T(1,128)S(1)}, u32[]{:S(2)}) copy-start(f32[1,17,257]{2,0,1:T(1,128)S(1)} %get-tuple-element.219) | copy-start | bytes 52432
  92.3 23.7 %copy-start.4 = (f32[1,17,257]{2,0,1:T(1,128)}, f32[1,17,257]{2,0,1:T(1,128)S(1)}, u32[]{:S(2)}) copy-start(f32[1,17,257]{2,0,1:T(1,128)S(1)} %get-tuple-element.140) | copy-start | bytes 52432
  92.3 23.7 %copy-start.6 = (f32[1,17,257]{2,0,1:T(1,128)}, f32[1,17,257]{2,0,1:T(1,128)S(1)}, u32[]{:S(2)}) copy-start(f32[1,17,257]{2,0,1:T(1,128)S(1)} %get-tuple-element.141) | copy-start | bytes 52432
  92.4 23.7 %copy-start.8 = (f32[1,17,257]{2,0,1:T(1,128)}, f32[1,17,257]{2,0,1:T(1,128)S(1)}, u32[]{:S(2)}) copy-start(f32[1,17,257]{2,0,1:T(1,128)S(1)} %get-tuple-element.142) | copy-start | bytes 52432
  93.1 6.5 %collective-permute-start.13 = (f32[4,1,18,258]{3,0,2,1:T(4,128)S(1)}, f32[4,1,18,258]{3,0,2,1:T(4,128)S(1)}, u32[]{:S(2)}, u32[]{:S(2)}) collective-permute-start(f32[4,1,18,258]{3,0,2,1:T(4,128)S(1)} %copy.246), channel_id=1, source_target_pairs={{1,0},{2,1},{3,2},{5,4},{6,5},{7,6},{9,8},{10,9},{11,10},{13,12},{... | collective-permute-start | bytes 222920 | tf_op jit(solution)/shard_map/ppermute | solution.py:16
  97.7 9.7 %copy-start.13 = (f32[1,17,257]{2,0,1:T(1,128)S(1)}, f32[1,17,257]{2,0,1:T(1,128)}, u32[]{:S(2)}) copy-start(f32[1,17,257]{2,0,1:T(1,128)} %get-tuple-element.99) | copy-start | bytes 52432
  97.7 9.7 %copy-start.14 = (f32[1,17,257]{2,0,1:T(1,128)S(1)}, f32[1,17,257]{2,0,1:T(1,128)}, u32[]{:S(2)}) copy-start(f32[1,17,257]{2,0,1:T(1,128)} %get-tuple-element.100) | copy-start | bytes 52432
  97.7 9.7 %copy-start.15 = (f32[1,17,257]{2,0,1:T(1,128)S(1)}, f32[1,17,257]{2,0,1:T(1,128)}, u32[]{:S(2)}) copy-start(f32[1,17,257]{2,0,1:T(1,128)} %get-tuple-element.104) | copy-start | bytes 52432
  97.7 9.7 %copy-start.16 = (f32[1,17,257]{2,0,1:T(1,128)S(1)}, f32[1,17,257]{2,0,1:T(1,128)}, u32[]{:S(2)}) copy-start(f32[1,17,257]{2,0,1:T(1,128)} %get-tuple-element.198) | copy-start | bytes 52432
  97.7 9.7 %copy-start.17 = (f32[1,17,257]{2,0,1:T(1,128)S(1)}, f32[1,17,257]{2,0,1:T(1,128)}, u32[]{:S(2)}) copy-start(f32[1,17,257]{2,0,1:T(1,128)} %get-tuple-element.199) | copy-start | bytes 52432
  97.7 9.7 %copy-start.18 = (f32[1,17,257]{2,0,1:T(1,128)S(1)}, f32[1,17,257]{2,0,1:T(1,128)}, u32[]{:S(2)}) copy-start(f32[1,17,257]{2,0,1:T(1,128)} %get-tuple-element.200) | copy-start | bytes 52432
  108.8 7.1 %copy-start.11 = (f32[1,17,257]{2,0,1:T(1,128)S(1)}, f32[1,17,257]{2,0,1:T(1,128)}, u32[]{:S(2)}) copy-start(f32[1,17,257]{2,0,1:T(1,128)} %get-tuple-element.72) | copy-start | bytes 52432
  108.9 7.1 %copy-start.12 = (f32[1,17,257]{2,0,1:T(1,128)S(1)}, f32[1,17,257]{2,0,1:T(1,128)}, u32[]{:S(2)}) copy-start(f32[1,17,257]{2,0,1:T(1,128)} %get-tuple-element.73) | copy-start | bytes 52432
  117.0 6.0 %copy-start.5 = (f32[1,17,257]{2,0,1:T(1,128)S(1)}, f32[1,17,257]{2,0,1:T(1,128)}, u32[]{:S(2)}) copy-start(f32[1,17,257]{2,0,1:T(1,128)} %copy-done.4) | copy-start | bytes 52432
  117.0 5.9 %copy-start.7 = (f32[1,17,257]{2,0,1:T(1,128)S(1)}, f32[1,17,257]{2,0,1:T(1,128)}, u32[]{:S(2)}) copy-start(f32[1,17,257]{2,0,1:T(1,128)} %copy-done.6) | copy-start | bytes 52432
  120.1 12.2 %copy-start.19 = (pred[16,256]{1,0:T(8,128)(4,1)S(1)}, pred[16,256]{1,0:T(8,128)(4,1)}, u32[]{:S(2)}) copy-start(pred[16,256]{1,0:T(8,128)(4,1)} %get-tuple-element.192) | copy-start | bytes 12292
  126.0 11.7 %copy-start.23 = (s32[2048]{0:T(1024)S(1)}, s32[2048]{0:T(1024)}, u32[]{:S(2)}) copy-start(s32[2048]{0:T(1024)} %pad_clamp_fusion) | copy-start | bytes 24580
  126.0 14.4 %copy-start.26 = (pred[1,9,128]{2,1,0:T(8,128)(4,1)S(1)}, pred[1,9,128]{2,1,0:T(8,128)(4,1)}, u32[]{:S(2)}) copy-start(pred[1,9,128]{2,1,0:T(8,128)(4,1)} %copy.299) | copy-start | bytes 3460
  126.0 33.5 %copy-start.3 = (f32[64,256]{1,0:T(8,128)S(1)}, f32[64,256]{1,0:T(8,128)}, u32[]{:S(2)}) copy-start(f32[64,256]{1,0:T(8,128)} %param.13) | copy-start | bytes 196612
  150.7 9.8 %collective-permute-start.14 = (f32[2,1,3,128]{3,0,2,1:T(2,128)S(1)}, f32[2,1,3,128]{3,0,2,1:T(2,128)S(1)}, u32[]{:S(2)}, u32[]{:S(2)}) collective-permute-start(f32[2,1,3,128]{3,0,2,1:T(2,128)S(1)} %get-tuple-element.184), channel_id=1, source_target_pairs={{0,16},{16,32},{32,48},{48,64},{64,80},{80,96},{96,112},{112,128},... | collective-permute-start | bytes 9224 | tf_op jit(solution)/shard_map/ppermute | solution.py:15
  157.5 6.1 %collective-permute-start.15 = (f32[2,1,3,128]{3,0,2,1:T(2,128)S(1)}, f32[2,1,3,128]{3,0,2,1:T(2,128)S(1)}, u32[]{:S(2)}, u32[]{:S(2)}) collective-permute-start(f32[2,1,3,128]{3,0,2,1:T(2,128)S(1)} %get-tuple-element.185), channel_id=1, source_target_pairs={{16,0},{32,16},{48,32},{64,48},{80,64},{96,80},{112,96},{128,112},... | collective-permute-start | bytes 9224 | tf_op jit(solution)/shard_map/ppermute | solution.py:16
  163.7 6.3 %collective-permute-start.16 = (f32[2,5,1,128]{3,0,2,1:T(2,128)S(1)}, f32[2,5,1,128]{3,0,2,1:T(2,128)S(1)}, u32[]{:S(2)}, u32[]{:S(2)}) collective-permute-start(f32[2,5,1,128]{3,0,2,1:T(2,128)S(1)} %get-tuple-element.180), channel_id=1, source_target_pairs={{0,4},{4,8},{8,12},{1,5},{5,9},{9,13},{2,6},{6,10},{10,14},{3,7},{... | collective-permute-start | bytes 15368 | tf_op jit(solution)/shard_map/ppermute | solution.py:15
  167.0 4.4 %collective-permute-start.17 = (f32[2,5,1,128]{3,0,2,1:T(2,128)S(1)}, f32[2,5,1,128]{3,0,2,1:T(2,128)S(1)}, u32[]{:S(2)}, u32[]{:S(2)}) collective-permute-start(f32[2,5,1,128]{3,0,2,1:T(2,128)S(1)} %get-tuple-element.181), channel_id=1, source_target_pairs={{4,0},{8,4},{12,8},{5,1},{9,5},{13,9},{6,2},{10,6},{14,10},{7,3},{... | collective-permute-start | bytes 15368 | tf_op jit(solution)/shard_map/ppermute | solution.py:16
